TPU v7x, 128 devices: a whole 4x4x4 slice. The times are simulated.
128 devices in a mesh: dp: 4 (over z), outer: 16 (over x, y), inner: 2 (over core).
Axes of the slice: x: 4, y: 4, z: 4, core: 2. Of those that a mesh axis runs over, the one named last changes fastest.
Arguments:
- tokens: bfloat16 [4096, 4096], P(('dp', 'outer', 'inner')), may hold values from -6 to 6
- expert_ids: int32 [4096, 8], P(('dp', 'outer', 'inner')), may hold values from 0 to 31, all different within a row; in each aligned block of 32 rows (0 to 31, 32 to 63, ...) at most 12 rows name the same one
- gate_values: float32 [4096, 8], P(('dp', 'outer', 'inner')), may hold values from 0.02 to 0.5
- upstream: bfloat16 [4096, 4096], P(('dp', 'outer', 'inner')), may hold values from -1.5 to 1.5
- w_gate: bfloat16 [32, 4096, 768], P(('outer', 'inner')), may hold values from -0.09375 to 0.09375
- w_up: bfloat16 [32, 4096, 768], P(('outer', 'inner')), may hold values from -0.09375 to 0.09375
- w_down: bfloat16 [32, 768, 4096], P(('outer', 'inner')), may hold values from -0.21875 to 0.21875
Outputs:
- output: bfloat16 [4096, 4096], P(('dp', 'outer', 'inner'))
- grad_tokens: bfloat16 [4096, 4096], P(('dp', 'outer', 'inner'))
- grad_gates: float32 [4096, 8], P(('dp', 'outer', 'inner'))
- grad_w_gate: bfloat16 [32, 4096, 768], P(('outer', 'inner'), 'dp')
- grad_w_up: bfloat16 [32, 4096, 768], P(('outer', 'inner'), 'dp')
- grad_w_down: bfloat16 [32, 768, 4096], P(('outer', 'inner'), None, 'dp')
Inputs may be any that keep to these rules, and one draw needn't show every extreme that they name: `expert_ids`: each token names 8 different experts. Among the 32 tokens of one device (aligned blocks of rows), no expert is named more than 12 times, a bound that some block reaches.
All inputs are finite; a program needn't handle non-finite values.
Results may differ from a plain program's by a relative error of at most 0.013.
Values may be sent and summed in bfloat16 or wider, within the bound.
No kernel may reach another device: no remote copies, remote signals or barrier semaphores. Data moves between devices by JAX's collectives and lax.ppermute only.
A program may use at most 192 MiB of HBM per device.

v0:
```python
import jax
import jax.numpy as jnp
from jax import lax
from jax.sharding import PartitionSpec as P


def contract_last(left, right):
    return lax.dot_general(
        left, right, (((1,), (1,)), ((), ())), preferred_element_type=jnp.float32
    )


def contract_first(left, right):
    return lax.dot_general(
        left, right, (((0,), (0,)), ((), ())), preferred_element_type=jnp.float32
    )


def expert_rows(rows_in, grads_in, gate_mat, up_mat, down_mat):
    gate_pre = jnp.dot(rows_in, gate_mat, preferred_element_type=jnp.float32)
    up_pre = jnp.dot(rows_in, up_mat, preferred_element_type=jnp.float32)
    sigma = jax.nn.sigmoid(gate_pre)
    silu_value = gate_pre * sigma
    hidden = (silu_value * up_pre).astype(jnp.bfloat16)
    expert_out = jnp.dot(hidden, down_mat, preferred_element_type=jnp.float32).astype(jnp.bfloat16)
    grad_hidden = contract_last(grads_in, down_mat)
    slope = sigma * (1.0 + gate_pre * (1.0 - sigma))
    grad_gate_pre = (grad_hidden * up_pre * slope).astype(jnp.bfloat16)
    grad_up_pre = (grad_hidden * silu_value).astype(jnp.bfloat16)
    pair_grad = (
        contract_last(grad_gate_pre, gate_mat) + contract_last(grad_up_pre, up_mat)
    ).astype(jnp.bfloat16)
    return (hidden, expert_out, grad_gate_pre, grad_up_pre, pair_grad)


def local(tokens, expert_ids, gate_values, upstream, w_gate, w_up, w_down):
    local_tokens = tokens.shape[0]
    width = tokens.shape[1]
    top_count = expert_ids.shape[1]
    ff_width = w_gate.shape[2]
    outer_count = lax.axis_size("outer")
    inner_count = lax.axis_size("inner")
    dp_count = lax.axis_size("dp")
    expert_count = outer_count * inner_count
    group = ("outer", "inner")
    me = lax.axis_index("outer") * inner_count + lax.axis_index("inner")
    group_tokens = expert_count * local_tokens
    capacity = min(local_tokens, 3 * local_tokens * top_count // (2 * expert_count))
    slot_total = expert_count * capacity
    ids_all = lax.all_gather(expert_ids, group, axis=0, tiled=True)
    gates_all = lax.all_gather(gate_values, group, axis=0, tiled=True)
    tokens_all = lax.all_gather(tokens, group, axis=0, tiled=True)
    upstream_all = lax.all_gather(upstream, group, axis=0, tiled=True)
    chosen = ids_all == me
    picked = jnp.any(chosen, axis=1)
    token_gate = jnp.sum(jnp.where(chosen, gates_all, 0.0), axis=1)
    position = jnp.cumsum(picked.astype(jnp.int32)) - 1
    token_slot = jnp.where(picked, position, slot_total)
    slot_token = (
        jnp.full((slot_total + 1,), group_tokens, jnp.int32)
        .at[token_slot]
        .set(jnp.arange(group_tokens, dtype=jnp.int32))[:slot_total]
    )
    token_pad = jnp.concatenate([tokens_all, jnp.zeros((1, width), jnp.bfloat16)], axis=0)
    upstream_pad = jnp.concatenate([upstream_all, jnp.zeros((1, width), jnp.bfloat16)], axis=0)
    gate_pad = jnp.concatenate([token_gate, jnp.zeros((1,), jnp.float32)], axis=0)
    rows_in = token_pad[slot_token]
    up_rows = upstream_pad[slot_token]
    grads_in = (gate_pad[slot_token][:, None] * up_rows.astype(jnp.float32)).astype(jnp.bfloat16)
    hidden, expert_out, grad_gate_pre, grad_up_pre, pair_grad = expert_rows(
        rows_in, grads_in, w_gate[0], w_up[0], w_down[0]
    )
    slot_gates_grad = jnp.sum(up_rows.astype(jnp.float32) * expert_out.astype(jnp.float32), axis=1)
    out_pad = jnp.concatenate([expert_out, jnp.zeros((1, width), jnp.bfloat16)], axis=0)
    back_pad = jnp.concatenate([pair_grad, jnp.zeros((1, width), jnp.bfloat16)], axis=0)
    gg_pad = jnp.concatenate([slot_gates_grad, jnp.zeros((1,), jnp.float32)], axis=0)
    out_share = (token_gate[:, None] * out_pad[token_slot].astype(jnp.float32)).astype(jnp.bfloat16)
    back_share = back_pad[token_slot]
    gg_share = jnp.where(chosen, gg_pad[token_slot][:, None], 0.0)
    output = lax.psum_scatter(out_share, group, scatter_dimension=0, tiled=True)
    grad_tokens = lax.psum_scatter(back_share, group, scatter_dimension=0, tiled=True)
    grad_gates = lax.psum_scatter(gg_share, group, scatter_dimension=0, tiled=True)
    piece = width // dp_count

    def spread_columns(block):
        return lax.all_to_all(
            block.reshape(slot_total, dp_count, piece),
            "dp",
            split_axis=1,
            concat_axis=0,
            tiled=True,
        ).reshape(dp_count * slot_total, piece)

    joined_grads = jnp.concatenate([grad_gate_pre, grad_up_pre], axis=1)
    rows_all = spread_columns(rows_in)
    grads_all = spread_columns(grads_in)
    joined_all = lax.all_gather(joined_grads, "dp", axis=0, tiled=True)
    hidden_all = lax.all_gather(hidden, "dp", axis=0, tiled=True)
    grad_joined = contract_first(rows_all, joined_all)
    grad_down = contract_first(hidden_all, grads_all)
    grad_w_gate = grad_joined[:, :ff_width].astype(jnp.bfloat16)[None]
    grad_w_up = grad_joined[:, ff_width:].astype(jnp.bfloat16)[None]
    grad_w_down = grad_down.astype(jnp.bfloat16)[None]
    return (output, grad_tokens, grad_gates, grad_w_gate, grad_w_up, grad_w_down)


def solution(mesh):
    placed = (
        P(("dp", "outer", "inner"), None),
        P(("dp", "outer", "inner"), None),
        P(("dp", "outer", "inner"), None),
        P(("dp", "outer", "inner"), None),
        P(("outer", "inner"), None, None),
        P(("outer", "inner"), None, None),
        P(("outer", "inner"), None, None),
    )
    return jax.shard_map(
        local,
        mesh=mesh,
        in_specs=placed,
        out_specs=(
            P(("dp", "outer", "inner"), None),
            P(("dp", "outer", "inner"), None),
            P(("dp", "outer", "inner"), None),
            P(("outer", "inner"), "dp", None),
            P(("outer", "inner"), "dp", None),
            P(("outer", "inner"), None, "dp"),
        ),
        check_vma=False,
    )
```

profile of v0, /device:TPU:0, one launch (start us, length us, event | category | flops | bytes accessed | tf_op | source)
XLA Modules:
  0.0 559.8 jit_solution(16613166208065047491)
XLA Ops:
  8.7 25.0 %all-gather = s32[32,32,8]{1,2,0:T(8,128)S(1)} all-gather(s32[1,32,8]{1,2,0:T(8,128)} %bitcast.73), channel_id=1, replica_groups=mesh['dp'=4,'outer'=16,'inner'=2] {'outer','inner'}, dimensions={0}, use_global_device_ids=true | all-gather | bytes 33792 | tf_op jit(solution)/shard_map/all_gather | solution.py:50
  34.5 24.0 %all-gather.1 = f32[32,32,8]{1,2,0:T(8,128)S(1)} all-gather(f32[1,32,8]{1,2,0:T(8,128)} %bitcast.74), channel_id=1, replica_groups=mesh['dp'=4,'outer'=16,'inner'=2] {'outer','inner'}, dimensions={0}, use_global_device_ids=true | all-gather | bytes 33792 | tf_op jit(solution)/shard_map/all_gather | solution.py:51
  66.1 7.7 %concatenate.24 = bf16[1025,4096]{1,0:T(8,128)(2,1)} pad(bf16[1024,4096]{1,0:T(8,128)(2,1)} %all-gather.9.cloned.1.call-done, bf16[]{:T(256)} %constant.7.clone.1), padding=0_1x0_0 | pad | bytes 16785410 | tf_op jit(solution)/shard_map/concatenate | solution.py:65
  73.8 12.8 %gather_fusion.3 = bf16[384,4096]{1,0:T(8,128)(2,1)} fusion(bf16[1025,4096]{1,0:T(8,128)(2,1)} %concatenate.24, s32[1024]{0:T(1024)S(1)} %pad_clamp_fusion), kind=kCustom, calls=%fused_computation.3 | custom fusion | bytes 6292992 | tf_op jit(solution)/shard_map/gather | solution.py:68
  86.6 34.0 %all-gather.7.cloned.1.call-done = bf16[1024,4096]{1,0:T(8,128)(2,1)} async-done(((bf16[32,4096]{1,0:T(8,128)(2,1)}), bf16[1024,4096]{1,0:T(8,128)(2,1)}) %all-gather.7.cloned.1.call-update) | async-done | bytes 8388624 | tf_op jit(solution)/shard_map/all_gather | solution.py:52
  120.6 7.7 %concatenate.21 = bf16[1025,4096]{1,0:T(8,128)(2,1)} pad(bf16[1024,4096]{1,0:T(8,128)(2,1)} %all-gather.7.cloned.1.call-done, bf16[]{:T(256)} %constant.7.clone.1), padding=0_1x0_0 | pad | bytes 16785410 | tf_op jit(solution)/shard_map/concatenate | solution.py:64
  128.3 12.5 %gather_fusion = bf16[384,4096]{1,0:T(8,128)(2,1)S(1)} fusion(bf16[1025,4096]{1,0:T(8,128)(2,1)} %concatenate.21, s32[1024]{0:T(1024)S(1)} %pad_clamp_fusion), kind=kCustom, calls=%fused_computation | custom fusion | bytes 6292992 | tf_op jit(solution)/shard_map/gather | solution.py:67
  140.8 6.5 %fusion.7 = f32[384,768]{1,0:T(8,128)S(1)} fusion(bf16[384,4096]{1,0:T(8,128)(2,1)S(1)} %gather_fusion, bf16[1,4096,768]{2,1,0:T(8,128)(2,1)} %param.12), kind=kOutput, calls=%fused_computation.16 | convolution fusion | flops 2415919104 | bytes 10616832 | tf_op jit(solution)/shard_map/dot_general | solution.py:21
  147.4 5.6 %fusion.1 = f32[384,768]{1,0:T(8,128)S(1)} fusion(bf16[1,768,4096]{2,1,0:T(8,128)(2,1)} %param.13, bf16[384,4096]{1,0:T(8,128)(2,1)S(1)} %copy-done.2, f32[384]{0:T(512)S(1)} %gather_fusion.2), kind=kOutput, calls=%fused_computation.10 | convolution fusion | flops 2420637696 | bytes 10618368 | tf_op jit(solution)/shard_map/dot_general | solution.py:8
  153.1 7.0 %multiply_convert_fusion.4 = (bf16[384,768]{1,0:T(8,128)(2,1)}, bf16[384,768]{1,0:T(8,128)(2,1)}, bf16[384,768]{1,0:T(8,128)(2,1)}) fusion(f32[384,768]{1,0:T(8,128)S(1)} %fusion.1, f32[384,768]{1,0:T(8,128)S(1)} %fusion.7, bf16[384,4096]{1,0:T(8,128)(2,1)S(1)} %gather_fusion, bf16[1,4096,768]{2,1,0:T(8,128)(2,1)} %param.11), kind=kOutput, calls=%fused_computation.36 | convolution fusion | flops 2420342784 | bytes 13565952 | tf_op jit(solution)/shard_map/dot_general | solution.py:20
  160.1 8.2 %multiply_reduce_fusion = (f32[384]{0:T(512)S(1)}, bf16[384,4096]{1,0:T(8,128)(2,1)}) fusion(bf16[384,4096]{1,0:T(8,128)(2,1)} %gather_fusion.3, bf16[384,768]{1,0:T(8,128)(2,1)} %get-tuple-element.12, bf16[1,768,4096]{2,1,0:T(8,128)(2,1)} %param.13), kind=kOutput, calls=%fused_computation.22 | convolution fusion | flops 2423782912 | bytes 13174272 | tf_op jit(solution)/shard_map/dot_general | solution.py:25
  168.3 6.9 %gather_fusion.5 = f32[1024]{0:T(1024)S(1)} fusion(f32[385]{0:T(512)S(1)} %pad_maximum_fusion.2, s32[1024]{0:T(1024)S(1)} %broadcast_clamp_fusion), kind=kCustom, calls=%fused_computation.5 | custom fusion | bytes 12288 | tf_op jit(solution)/shard_map/gather | solution.py:79
  183.0 7.3 %add_convert_fusion = bf16[384,4096]{1,0:T(8,128)(2,1)S(1)} fusion(f32[384,4096]{1,0:T(8,128)S(1)} %fusion.5, bf16[384,768]{1,0:T(8,128)(2,1)S(1)} %copy-done.4, bf16[1,4096,768]{2,1,0:T(8,128)(2,1)} %param.11), kind=kOutput, calls=%fused_computation.23 | convolution fusion | flops 2419064832 | bytes 16318464 | tf_op jit(solution)/shard_map/dot_general | solution.py:8
  190.6 7.8 %gather_fusion.4 = bf16[1024,4096]{1,0:T(8,128)(2,1)} fusion(bf16[385,4096]{1,0:T(8,128)(2,1)S(1)} %concatenate.25, s32[1024]{0:T(1024)S(1)} %broadcast_clamp_fusion), kind=kCustom, calls=%fused_computation.4 | custom fusion | bytes 16781312 | tf_op jit(solution)/shard_map/gather | solution.py:78
  200.6 7.8 %gather_fusion.1 = bf16[1024,4096]{1,0:T(8,128)(2,1)} fusion(bf16[385,4096]{1,0:T(8,128)(2,1)S(1)} %concatenate.22, s32[1024]{0:T(1024)S(1)} %broadcast_clamp_fusion), kind=kCustom, calls=%fused_computation.1 | custom fusion | bytes 16781312 | tf_op jit(solution)/shard_map/gather | solution.py:77
  208.4 10.0 %multiply_convert_fusion = bf16[1024,4096]{1,0:T(8,128)(2,1)} fusion(bf16[1024,4096]{1,0:T(8,128)(2,1)} %gather_fusion.1, f32[1024]{0:T(1024)S(1)} %select_reduce_fusion), kind=kLoop, calls=%fused_computation.7 | loop fusion | flops 12582912 | bytes 16781312 | tf_op jit(solution)/shard_map/convert_element_type | solution.py:77
  230.9 36.1 %all-to-all-done.1 = bf16[384,4,1024]{2,0,1:T(8,128)(2,1)} async-done(((bf16[384,4,1024]{2,0,1:T(8,128)(2,1)}), bf16[384,4,1024]{2,0,1:T(8,128)(2,1)}, u32[]{:S(2)}, u32[]{:S(2)}) %all-to-all-start.1) | async-done | bytes 3145760 | tf_op jit(solution)/shard_map/all_to_all | solution.py:86
  272.4 27.9 %all-gather.13.cloned.1.call-done = bf16[1536,768]{1,0:T(8,128)(2,1)} async-done(((bf16[384,768]{1,0:T(8,128)(2,1)}), bf16[1536,768]{1,0:T(8,128)(2,1)}) %all-gather.13.cloned.1.call-update) | async-done | bytes 2359312 | tf_op jit(solution)/shard_map/all_gather | solution.py:98
  300.3 6.4 %fusion.20 = bf16[1,768,1024]{2,1,0:T(8,128)(2,1)} fusion(bf16[1536,768]{1,0:T(8,128)(2,1)} %all-gather.13.cloned.1.call-done, bf16[1536,1024]{1,0:T(8,128)(2,1)} %bitcast.14), kind=kOutput, calls=%fused_computation.33 | convolution fusion | flops 2416705536 | bytes 7077888 | tf_op jit(solution)/shard_map/dot_general | solution.py:14
  306.7 17.0 %all-to-all-done = bf16[384,4,1024]{2,0,1:T(8,128)(2,1)S(1)} async-done(((bf16[384,4,1024]{2,0,1:T(8,128)(2,1)}), bf16[384,4,1024]{2,0,1:T(8,128)(2,1)S(1)}, u32[]{:S(2)}, u32[]{:S(2)}) %all-to-all-start) | async-done | bytes 3145760 | tf_op jit(solution)/shard_map/all_to_all | solution.py:86
  323.7 35.8 %all-gather.11.cloned.1.call-done = bf16[1536,1536]{1,0:T(8,128)(2,1)} async-done(((bf16[384,1536]{1,0:T(8,128)(2,1)}), bf16[1536,1536]{1,0:T(8,128)(2,1)}) %all-gather.11.cloned.1.call-update) | async-done | bytes 4718608 | tf_op jit(solution)/shard_map/all_gather | solution.py:97
  359.5 7.7 %convolution_convert_fusion = bf16[1024,1536]{1,0:T(8,128)(2,1)S(1)} fusion(bf16[1536,1024]{1,0:T(8,128)(2,1)S(1)} %bitcast.69, bf16[1536,1536]{1,0:T(8,128)(2,1)} %all-gather.11.cloned.1.call-done), kind=kOutput, calls=%fused_computation.26 | convolution fusion | flops 4833411072 | bytes 11010048 | tf_op jit(solution)/shard_map/dot_general | solution.py:14
  369.1 86.9 %reduce-scatter.8.cloned.1.call-done = bf16[32,4096]{1,0:T(8,128)(2,1)} async-done(((bf16[1024,4096]{1,0:T(8,128)(2,1)}), bf16[32,4096]{1,0:T(8,128)(2,1)}) %reduce-scatter.8.cloned.1.call-update) | async-done | bytes 262160 | tf_op jit(solution)/shard_map/reduce_scatter | solution.py:81
  456.0 96.7 %reduce-scatter.6.cloned.1.call-done = bf16[32,4096]{1,0:T(8,128)(2,1)} async-done(((bf16[1024,4096]{1,0:T(8,128)(2,1)}), bf16[32,4096]{1,0:T(8,128)(2,1)}) %reduce-scatter.6.cloned.1.call-update) | async-done | bytes 262160 | tf_op jit(solution)/shard_map/reduce_scatter | solution.py:80
  (64 shorter events, 39.7 us)
Async XLA Ops:
  7.2 58.9 %all-gather.9.cloned.1.call-start = ((), (), s32[]{:S(2)}) async-start(), calls=%async_computation.7 | async-start | bytes 8650752 | tf_op jit(solution)/shard_map/all_gather | solution.py:53
  7.9 112.7 %all-gather.7.cloned.1.call-start = ((), (), s32[]{:S(2)}) async-start(), calls=%async_computation.5 | async-start | bytes 8650752 | tf_op jit(solution)/shard_map/all_gather | solution.py:52
  8.6 262.4 %reduce-scatter.10.cloned.1.call-start = ((), (), s32[]{:S(2)}) async-start(), calls=%async_computation.11 | async-start | bytes 540672
  140.8 12.2 %copy-start = (bf16[384,4096]{1,0:T(8,128)(2,1)}, bf16[384,4096]{1,0:T(8,128)(2,1)S(1)}, u32[]{:S(2)}) copy-start(bf16[384,4096]{1,0:T(8,128)(2,1)S(1)} %gather_fusion) | copy-start | bytes 9437188
  140.8 6.6 %copy-start.2 = (bf16[384,4096]{1,0:T(8,128)(2,1)S(1)}, bf16[384,4096]{1,0:T(8,128)(2,1)}, u32[]{:S(2)}) copy-start(bf16[384,4096]{1,0:T(8,128)(2,1)} %gather_fusion.3) | copy-start | bytes 9437188
  168.3 8.6 %copy-start.4 = (bf16[384,768]{1,0:T(8,128)(2,1)S(1)}, bf16[384,768]{1,0:T(8,128)(2,1)}, u32[]{:S(2)}) copy-start(bf16[384,768]{1,0:T(8,128)(2,1)} %get-tuple-element.10) | copy-start | bytes 1769476
  168.3 8.6 %copy-start.5 = (bf16[384,768]{1,0:T(8,128)(2,1)S(1)}, bf16[384,768]{1,0:T(8,128)(2,1)}, u32[]{:S(2)}) copy-start(bf16[384,768]{1,0:T(8,128)(2,1)} %get-tuple-element.11) | copy-start | bytes 1769476
  176.2 124.1 %all-gather.13.cloned.1.call-start = ((), (), s32[]{:S(2)}) async-start(), calls=%async_computation.10 | async-start | bytes 2949120 | tf_op jit(solution)/shard_map/all_gather | solution.py:98
  176.8 182.7 %all-gather.11.cloned.1.call-start = ((), (), s32[]{:S(2)}) async-start(), calls=%async_computation.9 | async-start | bytes 5898240 | tf_op jit(solution)/shard_map/all_gather | solution.py:97
  178.0 278.0 %reduce-scatter.8.cloned.1.call-start = ((), (), s32[]{:S(2)}) async-start(), calls=%async_computation.8 | async-start | bytes 8650752 | tf_op jit(solution)/shard_map/reduce_scatter | solution.py:81
  198.4 354.4 %reduce-scatter.6.cloned.1.call-start = ((), (), s32[]{:S(2)}) async-start(), calls=%async_computation.6 | async-start | bytes 8650752 | tf_op jit(solution)/shard_map/reduce_scatter | solution.py:80
  218.4 1.9 copy-start.3
  223.8 5.0 copy-start.1
  223.8 43.3 %all-to-all-start.1 = ((bf16[384,4,1024]{2,0,1:T(8,128)(2,1)}), bf16[384,4,1024]{2,0,1:T(8,128)(2,1)}, u32[]{:S(2)}, u32[]{:S(2)}) async-start(bf16[384,4,1024]{2,0,1:T(8,128)(2,1)} %fusion), calls=%async_computation.3 | async-start | bytes 6291456 | tf_op jit(solution)/shard_map/all_to_all | solution.py:86
  267.1 56.6 %all-to-all-start = ((bf16[384,4,1024]{2,0,1:T(8,128)(2,1)}), bf16[384,4,1024]{2,0,1:T(8,128)(2,1)S(1)}, u32[]{:S(2)}, u32[]{:S(2)}) async-start(bf16[384,4,1024]{2,0,1:T(8,128)(2,1)} %bitcast.68), calls=%async_computation.2 | async-start | bytes 6291456 | tf_op jit(solution)/shard_map/all_to_all | solution.py:86
Sparse Core Ops, SparseCore 0:
  10.3 55.5 all-gather.8
  68.1 52.4 all-gather.6
  176.4 76.5 reduce-scatter.9
  255.0 45.2 all-gather.12
  302.4 57.0 all-gather.10
  363.7 92.2 reduce-scatter.7
  460.8 91.9 reduce-scatter.5
where the time goes:
time: 564 us; the launch traced here: 560 us
  waiting for transfers between devices  337 us (60%)
  local copies, waits for them, and re-layouts  81.7 us (14%)
  matrix products  53.7 us (10%)
  blocking collectives  49 us (9%)
  other arithmetic  15.1 us (3%)
  between operations  14.6 us (3%)
  starting transfers between devices  9.13 us (2%)
    reduce_scatter x1, waiting for transfers between devices, local(): output = lax.psum_scatter(out_share, group, scatter_dimension=0, tiled=True)  96.7 us
    reduce_scatter x1, waiting for transfers between devices, local(): lax.psum_scatter(back_share, group, scatter_dimension=0, tiled=True)  86.9 us
    all_to_all x2, waiting for transfers between devices, spread_columns(): lax.all_to_all(block.reshape(slot_total, dp_count, piece), 'dp', split_ax...  53.1 us
    all_gather x1, waiting for transfers between devices, local(): joined_all = lax.all_gather(joined_grads, 'dp', axis=0, tiled=True)  35.8 us
    all_gather x1, waiting for transfers between devices, local(): tokens_all = lax.all_gather(tokens, group, axis=0, tiled=True)  34 us
    all_gather x1, waiting for transfers between devices, local(): hidden_all = lax.all_gather(hidden, 'dp', axis=0, tiled=True)  27.9 us
    all_gather x1, blocking collectives, local(): ids_all = lax.all_gather(expert_ids, group, axis=0, tiled=True)  25 us
    all_gather x1, blocking collectives, local(): gates_all = lax.all_gather(gate_values, group, axis=0, tiled=True)  24 us
  transfers between devices with their start and end apart: 9, of which 7 were waited for; matrix products, arithmetic and copies ran while one was open for 17% of the time, Pallas kernels for 0%

commit v1 on v0

--- a/solution.py
+++ b/solution.py
@@ -95,7 +95,12 @@
     rows_all = spread_columns(rows_in)
     grads_all = spread_columns(grads_in)
     joined_all = lax.all_gather(joined_grads, "dp", axis=0, tiled=True)
-    hidden_all = lax.all_gather(hidden, "dp", axis=0, tiled=True)
+    ring = [hidden]
+    for hop in range(3):
+        ring.append(lax.ppermute(ring[-1], "dp", [(dev, (dev + 1) % 4) for dev in range(4)]))
+    hidden_all = jnp.roll(
+        jnp.concatenate(ring[::-1], axis=0), (lax.axis_index("dp") + 1) * ring[0].shape[0], axis=0
+    )
     grad_joined = contract_first(rows_all, joined_all)
     grad_down = contract_first(hidden_all, grads_all)
     grad_w_gate = grad_joined[:, :ff_width].astype(jnp.bfloat16)[None]

time: 564 us -> 543 us (0.963)
  waiting for transfers between devices: 337 us -> 308 us
  local copies, waits for them, and re-layouts: 81.7 us -> 90.5 us
    ppermute x0 -> x3, waiting for transfers between devices: none -> 138 us  [local(): lax.ppermute(ring[-1], 'dp', [(dev, (dev + 1) % 4) for dev in range(4)])]
    reduce_scatter x1, waiting for transfers between devices: 96.7 us -> 38.8 us  [local(): output = lax.psum_scatter(out_share, group, scatter_dimension=0, tiled=True)]
    all_to_all x2, waiting for transfers between devices: 53.1 us -> 0.01 us  [spread_columns(): lax.all_to_all(block.reshape(slot_total, dp_count, piece), 'dp', split_ax...]
    all_gather x1, waiting for transfers between devices: 35.8 us -> 0.01 us  [local(): joined_all = lax.all_gather(joined_grads, 'dp', axis=0, tiled=True)]
    all_gather x1 -> x0, waiting for transfers between devices: 27.9 us -> none  [local(): hidden_all = lax.all_gather(hidden, 'dp', axis=0, tiled=True)]
    reduce_scatter x1, waiting for transfers between devices: 86.9 us -> 96.7 us  [local(): lax.psum_scatter(back_share, group, scatter_dimension=0, tiled=True)]
    unnamed x15 -> x34, local copies, waits for them, and re-layouts: 4.39 us -> 13.3 us
  transfers between devices with their start and end apart: 9 -> 11, of which waited for: 7 -> 6; matrix products, arithmetic and copies ran while one was open for 17% -> 19% of each run, Pallas kernels for 0% -> 0%
where the time goes in v1:
time: 543 us; the launch traced here: 538 us
  waiting for transfers between devices  308 us (57%)
  local copies, waits for them, and re-layouts  90.5 us (17%)
  matrix products  49.2 us (9%)
  blocking collectives  49 us (9%)
  other arithmetic  15.2 us (3%)
  between operations  14.7 us (3%)
  starting transfers between devices  11.7 us (2%)
    ppermute x3, waiting for transfers between devices, local(): lax.ppermute(ring[-1], 'dp', [(dev, (dev + 1) % 4) for dev in range(4)])  138 us
    reduce_scatter x1, waiting for transfers between devices, local(): lax.psum_scatter(back_share, group, scatter_dimension=0, tiled=True)  96.7 us
    reduce_scatter x1, waiting for transfers between devices, local(): output = lax.psum_scatter(out_share, group, scatter_dimension=0, tiled=True)  38.8 us
    all_gather x1, waiting for transfers between devices, local(): tokens_all = lax.all_gather(tokens, group, axis=0, tiled=True)  33.8 us
    all_gather x1, blocking collectives, local(): ids_all = lax.all_gather(expert_ids, group, axis=0, tiled=True)  25 us
    all_gather x1, blocking collectives, local(): gates_all = lax.all_gather(gate_values, group, axis=0, tiled=True)  24 us
    dot_general x3, matrix products, contract_last(): lax.dot_general(left, right, (((1,), (1,)), ((), ())), preferred_element_...  18.1 us
    dot_general x2, matrix products, contract_first(): lax.dot_general(left, right, (((0,), (0,)), ((), ())), preferred_element_...  13.4 us
  transfers between devices with their start and end apart: 11, of which 6 were waited for; matrix products, arithmetic and copies ran while one was open for 19% of the time, Pallas kernels for 0%

profile of v1, /device:TPU:0, one launch (start us, length us, event | category | flops | bytes accessed | tf_op | source)
XLA Modules:
  0.0 538.5 jit_solution(14838208594582806953)
XLA Ops:
  8.7 25.0 %all-gather = s32[32,32,8]{1,2,0:T(8,128)S(1)} all-gather(s32[1,32,8]{1,2,0:T(8,128)} %bitcast.72), channel_id=1, replica_groups=mesh['dp'=4,'outer'=16,'inner'=2] {'outer','inner'}, dimensions={0}, use_global_device_ids=true | all-gather | bytes 33792 | tf_op jit(solution)/shard_map/all_gather | solution.py:50
  34.5 24.0 %all-gather.1 = f32[32,32,8]{1,2,0:T(8,128)S(1)} all-gather(f32[1,32,8]{1,2,0:T(8,128)} %bitcast.73), channel_id=1, replica_groups=mesh['dp'=4,'outer'=16,'inner'=2] {'outer','inner'}, dimensions={0}, use_global_device_ids=true | all-gather | bytes 33792 | tf_op jit(solution)/shard_map/all_gather | solution.py:51
  66.3 7.8 %concatenate.30 = bf16[1025,4096]{1,0:T(8,128)(2,1)} pad(bf16[1024,4096]{1,0:T(8,128)(2,1)} %all-gather.8.cloned.1.call-done, bf16[]{:T(256)} %constant.24.clone.1), padding=0_1x0_0 | pad | bytes 16785410 | tf_op jit(solution)/shard_map/concatenate | solution.py:65
  74.0 12.8 %gather_fusion.3 = bf16[384,4096]{1,0:T(8,128)(2,1)} fusion(bf16[1025,4096]{1,0:T(8,128)(2,1)} %concatenate.30, s32[1024]{0:T(1024)S(1)} %pad_clamp_fusion), kind=kCustom, calls=%fused_computation.3 | custom fusion | bytes 6292992 | tf_op jit(solution)/shard_map/gather | solution.py:68
  86.8 33.8 %all-gather.6.cloned.1.call-done = bf16[1024,4096]{1,0:T(8,128)(2,1)} async-done(((bf16[32,4096]{1,0:T(8,128)(2,1)}), bf16[1024,4096]{1,0:T(8,128)(2,1)}) %all-gather.6.cloned.1.call-update) | async-done | bytes 8388624 | tf_op jit(solution)/shard_map/all_gather | solution.py:52
  120.6 7.7 %concatenate.27 = bf16[1025,4096]{1,0:T(8,128)(2,1)} pad(bf16[1024,4096]{1,0:T(8,128)(2,1)} %all-gather.6.cloned.1.call-done, bf16[]{:T(256)} %constant.24.clone.1), padding=0_1x0_0 | pad | bytes 16785410 | tf_op jit(solution)/shard_map/concatenate | solution.py:64
  128.3 12.2 %gather_fusion = bf16[384,4096]{1,0:T(8,128)(2,1)S(1)} fusion(bf16[1025,4096]{1,0:T(8,128)(2,1)} %concatenate.27, s32[1024]{0:T(1024)S(1)} %pad_clamp_fusion), kind=kCustom, calls=%fused_computation | custom fusion | bytes 6292992 | tf_op jit(solution)/shard_map/gather | solution.py:67
  140.5 6.5 %fusion.7 = f32[384,768]{1,0:T(8,128)S(1)} fusion(bf16[384,4096]{1,0:T(8,128)(2,1)S(1)} %gather_fusion, bf16[1,4096,768]{2,1,0:T(8,128)(2,1)} %param.12), kind=kOutput, calls=%fused_computation.16 | convolution fusion | flops 2415919104 | bytes 10616832 | tf_op jit(solution)/shard_map/dot_general | solution.py:21
  147.1 5.8 %fusion.1 = f32[384,768]{1,0:T(8,128)S(1)} fusion(bf16[1,768,4096]{2,1,0:T(8,128)(2,1)} %param.13, bf16[384,4096]{1,0:T(8,128)(2,1)S(1)} %copy-done.2, f32[384]{0:T(512)S(1)} %gather_fusion.2), kind=kOutput, calls=%fused_computation.10 | convolution fusion | flops 2420637696 | bytes 10618368 | tf_op jit(solution)/shard_map/dot_general | solution.py:8
  152.9 6.9 %multiply_convert_fusion.4 = (bf16[384,768]{1,0:T(8,128)(2,1)}, bf16[384,768]{1,0:T(8,128)(2,1)}, bf16[384,768]{1,0:T(8,128)(2,1)S(1)}) fusion(f32[384,768]{1,0:T(8,128)S(1)} %fusion.1, f32[384,768]{1,0:T(8,128)S(1)} %fusion.7, bf16[384,4096]{1,0:T(8,128)(2,1)S(1)} %gather_fusion, bf16[1,4096,768]{2,1,0:T(8,128)(2,1)} %param.11), kind=kOutput, calls=%fused_computation.38 | convolution fusion | flops 2420342784 | bytes 13565952 | tf_op jit(solution)/shard_map/dot_general | solution.py:20
  164.1 6.9 %gather_fusion.5 = f32[1024]{0:T(1024)S(1)} fusion(f32[385]{0:T(512)S(1)} %pad_maximum_fusion.2, s32[1024]{0:T(1024)S(1)} %broadcast_clamp_fusion), kind=kCustom, calls=%fused_computation.5 | custom fusion | bytes 12288 | tf_op jit(solution)/shard_map/gather | solution.py:79
  175.5 7.8 %gather_fusion.1 = bf16[1024,4096]{1,0:T(8,128)(2,1)} fusion(bf16[385,4096]{1,0:T(8,128)(2,1)S(1)} %concatenate.28, s32[1024]{0:T(1024)S(1)} %broadcast_clamp_fusion), kind=kCustom, calls=%fused_computation.1 | custom fusion | bytes 16781312 | tf_op jit(solution)/shard_map/gather | solution.py:77
  183.3 10.0 %multiply_convert_fusion = bf16[1024,4096]{1,0:T(8,128)(2,1)} fusion(bf16[1024,4096]{1,0:T(8,128)(2,1)} %gather_fusion.1, f32[1024]{0:T(1024)S(1)} %select_reduce_fusion), kind=kLoop, calls=%fused_computation.7 | loop fusion | flops 12582912 | bytes 16781312 | tf_op jit(solution)/shard_map/convert_element_type | solution.py:77
  194.4 5.0 fusion.5
  199.4 7.3 %add_convert_fusion = bf16[384,4096]{1,0:T(8,128)(2,1)S(1)} fusion(f32[384,4096]{1,0:T(8,128)S(1)} %fusion.5, bf16[384,768]{1,0:T(8,128)(2,1)S(1)} %copy-done.7, bf16[1,4096,768]{2,1,0:T(8,128)(2,1)} %param.11), kind=kOutput, calls=%fused_computation.23 | convolution fusion | flops 2419064832 | bytes 16318464 | tf_op jit(solution)/shard_map/dot_general | solution.py:8
  207.0 7.7 %gather_fusion.4 = bf16[1024,4096]{1,0:T(8,128)(2,1)} fusion(bf16[385,4096]{1,0:T(8,128)(2,1)S(1)} %concatenate.31, s32[1024]{0:T(1024)S(1)} %broadcast_clamp_fusion), kind=kCustom, calls=%fused_computation.4 | custom fusion | bytes 16781312 | tf_op jit(solution)/shard_map/gather | solution.py:78
  220.1 4.9 all-to-all-start.1
  227.1 60.1 %collective-permute-done = bf16[384,768]{1,0:T(8,128)(2,1)} collective-permute-done((bf16[384,768]{1,0:T(8,128)(2,1)}, bf16[384,768]{1,0:T(8,128)(2,1)}, u32[]{:S(2)}, u32[]{:S(2)}) %collective-permute-start) | collective-permute-done | bytes 589856 | tf_op jit(solution)/shard_map/ppermute | solution.py:100
  293.9 23.6 %collective-permute-done.1 = bf16[384,768]{1,0:T(8,128)(2,1)} collective-permute-done((bf16[384,768]{1,0:T(8,128)(2,1)}, bf16[384,768]{1,0:T(8,128)(2,1)}, u32[]{:S(2)}, u32[]{:S(2)}) %collective-permute-start.1) | collective-permute-done | bytes 589856 | tf_op jit(solution)/shard_map/ppermute | solution.py:100
  318.9 53.8 %collective-permute-done.2 = bf16[384,768]{1,0:T(8,128)(2,1)} collective-permute-done((bf16[384,768]{1,0:T(8,128)(2,1)}, bf16[384,768]{1,0:T(8,128)(2,1)}, u32[]{:S(2)}, u32[]{:S(2)}) %collective-permute-start.2) | collective-permute-done | bytes 589856 | tf_op jit(solution)/shard_map/ppermute | solution.py:100
  380.7 5.7 %fusion.25 = bf16[1,768,1024]{2,1,0:T(8,128)(2,1)} fusion(bf16[1536,1024]{1,0:T(8,128)(2,1)} %bitcast.14, bf16[3072,768]{1,0:T(8,128)(2,1)S(1)} %constant_dynamic-update-slice_fusion, s32[]{:T(128)S(6)} %select_n.56), kind=kOutput, calls=%fused_computation.35 | convolution fusion | flops 2416705536 | bytes 7077892 | tf_op jit(solution)/shard_map/dot_general | solution.py:14
  386.4 7.7 %convolution_convert_fusion = bf16[1024,1536]{1,0:T(8,128)(2,1)S(1)} fusion(bf16[1536,1024]{1,0:T(8,128)(2,1)S(1)} %bitcast.68, bf16[1536,1536]{1,0:T(8,128)(2,1)} %all-gather.10.cloned.1.call-done), kind=kOutput, calls=%fused_computation.26 | convolution fusion | flops 4833411072 | bytes 11010048 | tf_op jit(solution)/shard_map/dot_general | solution.py:14
  396.0 38.8 %reduce-scatter.6.cloned.1.call-done = bf16[32,4096]{1,0:T(8,128)(2,1)} async-done(((bf16[1024,4096]{1,0:T(8,128)(2,1)}), bf16[32,4096]{1,0:T(8,128)(2,1)}) %reduce-scatter.6.cloned.1.call-update) | async-done | bytes 262160 | tf_op jit(solution)/shard_map/reduce_scatter | solution.py:80
  434.7 96.7 %reduce-scatter.8.cloned.1.call-done = bf16[32,4096]{1,0:T(8,128)(2,1)} async-done(((bf16[1024,4096]{1,0:T(8,128)(2,1)}), bf16[32,4096]{1,0:T(8,128)(2,1)}) %reduce-scatter.8.cloned.1.call-update) | async-done | bytes 262160 | tf_op jit(solution)/shard_map/reduce_scatter | solution.py:81
  (88 shorter events, 45.2 us)
Async XLA Ops:
  7.2 59.1 %all-gather.8.cloned.1.call-start = ((), (), s32[]{:S(2)}) async-start(), calls=%async_computation.7 | async-start | bytes 8650752 | tf_op jit(solution)/shard_map/all_gather | solution.py:53
  7.9 112.7 %all-gather.6.cloned.1.call-start = ((), (), s32[]{:S(2)}) async-start(), calls=%async_computation.5 | async-start | bytes 8650752 | tf_op jit(solution)/shard_map/all_gather | solution.py:52
  8.6 308.9 %reduce-scatter.10.cloned.1.call-start = ((), (), s32[]{:S(2)}) async-start(), calls=%async_computation.10 | async-start | bytes 540672
  140.5 12.4 %copy-start = (bf16[384,4096]{1,0:T(8,128)(2,1)}, bf16[384,4096]{1,0:T(8,128)(2,1)S(1)}, u32[]{:S(2)}) copy-start(bf16[384,4096]{1,0:T(8,128)(2,1)S(1)} %gather_fusion) | copy-start | bytes 9437188
  140.5 6.6 %copy-start.2 = (bf16[384,4096]{1,0:T(8,128)(2,1)S(1)}, bf16[384,4096]{1,0:T(8,128)(2,1)}, u32[]{:S(2)}) copy-start(bf16[384,4096]{1,0:T(8,128)(2,1)} %gather_fusion.3) | copy-start | bytes 9437188
  147.1 12.8 %slice-start = ((s8[6291456]{0:T(1024)(128)(4,1)}), s8[4194304]{0:T(1024)(128)(4,1)S(1)}, s32[]{:S(2)}) async-start(s8[6291456]{0:T(1024)(128)(4,1)} %bitcast.74), calls=%async_computation.11 | async-start | bytes 8388608
  152.9 7.0 %slice-start.1 = ((s8[6291456]{0:T(1024)(128)(4,1)}), s8[2097152]{0:T(1024)(128)(4,1)S(1)}, s32[]{:S(2)}) async-start(s8[6291456]{0:T(1024)(128)(4,1)} %bitcast.74), calls=%async_computation.12 | async-start | bytes 4194304
  159.9 4.3 copy-start.4
  164.1 8.0 %copy-start.6 = (bf16[384,768]{1,0:T(8,128)(2,1)S(1)}, bf16[384,768]{1,0:T(8,128)(2,1)}, u32[]{:S(2)}) copy-start(bf16[384,768]{1,0:T(8,128)(2,1)} %get-tuple-element.10) | copy-start | bytes 1769476
  164.1 8.0 %copy-start.8 = (bf16[384,768]{1,0:T(8,128)(2,1)S(1)}, bf16[384,768]{1,0:T(8,128)(2,1)}, u32[]{:S(2)}) copy-start(bf16[384,768]{1,0:T(8,128)(2,1)} %get-tuple-element.11) | copy-start | bytes 1769476
  172.1 214.3 %all-gather.10.cloned.1.call-start = ((), (), s32[]{:S(2)}) async-start(), calls=%async_computation.9 | async-start | bytes 5898240 | tf_op jit(solution)/shard_map/all_gather | solution.py:97
  173.3 261.5 %reduce-scatter.6.cloned.1.call-start = ((), (), s32[]{:S(2)}) async-start(), calls=%async_computation.6 | async-start | bytes 8650752 | tf_op jit(solution)/shard_map/reduce_scatter | solution.py:80
  193.3 1.1 copy-start.9
  193.3 6.0 %copy-start.7 = (bf16[384,768]{1,0:T(8,128)(2,1)S(1)}, bf16[384,768]{1,0:T(8,128)(2,1)}, u32[]{:S(2)}) copy-start(bf16[384,768]{1,0:T(8,128)(2,1)} %get-tuple-element.10) | copy-start | bytes 1769476
  193.3 338.1 %reduce-scatter.8.cloned.1.call-start = ((), (), s32[]{:S(2)}) async-start(), calls=%async_computation.8 | async-start | bytes 8650752 | tf_op jit(solution)/shard_map/reduce_scatter | solution.py:81
  214.7 1.9 copy-start.3
  220.1 67.1 %copy-start.1 = (bf16[384,4096]{1,0:T(8,128)(2,1)S(1)}, bf16[384,4096]{1,0:T(8,128)(2,1)}, u32[]{:S(2)}) copy-start(bf16[384,4096]{1,0:T(8,128)(2,1)} %copy-done) | copy-start | bytes 9437188
  220.1 69.2 %all-to-all-start.1 = ((bf16[384,4,1024]{2,0,1:T(8,128)(2,1)}), bf16[384,4,1024]{2,0,1:T(8,128)(2,1)}, u32[]{:S(2)}, u32[]{:S(2)}) async-start(bf16[384,4,1024]{2,0,1:T(8,128)(2,1)} %fusion), calls=%async_computation.3 | async-start | bytes 6291456 | tf_op jit(solution)/shard_map/all_to_all | solution.py:86
  225.1 62.1 %collective-permute-start = (bf16[384,768]{1,0:T(8,128)(2,1)}, bf16[384,768]{1,0:T(8,128)(2,1)}, u32[]{:S(2)}, u32[]{:S(2)}) collective-permute-start(bf16[384,768]{1,0:T(8,128)(2,1)} %copy-done.4), channel_id=1, source_target_pairs={{0,32},{32,64},{64,96},{96,0},{1,33},{33,65},{65,97},{97,1},{2,34}... | collective-permute-start | bytes 1769480 | tf_op jit(solution)/shard_map/ppermute | solution.py:100
  287.2 30.3 %collective-permute-start.1 = (bf16[384,768]{1,0:T(8,128)(2,1)}, bf16[384,768]{1,0:T(8,128)(2,1)}, u32[]{:S(2)}, u32[]{:S(2)}) collective-permute-start(bf16[384,768]{1,0:T(8,128)(2,1)} %collective-permute-done), channel_id=1, source_target_pairs={{0,32},{32,64},{64,96},{96,0},{1,33},{33,65},{65,97},{97,1},{2,34}... | collective-permute-start | bytes 1769480 | tf_op jit(solution)/shard_map/ppermute | solution.py:100
  289.3 97.1 %all-to-all-start = ((bf16[384,4,1024]{2,0,1:T(8,128)(2,1)}), bf16[384,4,1024]{2,0,1:T(8,128)(2,1)S(1)}, u32[]{:S(2)}, u32[]{:S(2)}) async-start(bf16[384,4,1024]{2,0,1:T(8,128)(2,1)} %bitcast.67), calls=%async_computation.2 | async-start | bytes 6291456 | tf_op jit(solution)/shard_map/all_to_all | solution.py:86
  317.5 55.2 %collective-permute-start.2 = (bf16[384,768]{1,0:T(8,128)(2,1)}, bf16[384,768]{1,0:T(8,128)(2,1)}, u32[]{:S(2)}, u32[]{:S(2)}) collective-permute-start(bf16[384,768]{1,0:T(8,128)(2,1)} %collective-permute-done.1), channel_id=1, source_target_pairs={{0,32},{32,64},{64,96},{96,0},{1,33},{33,65},{65,97},{97,1},{2,34}... | collective-permute-start | bytes 1769480 | tf_op jit(solution)/shard_map/ppermute | solution.py:100
  318.9 61.8 %copy-start.5 = (bf16[384,768]{1,0:T(8,128)(2,1)S(1)}, bf16[384,768]{1,0:T(8,128)(2,1)}, u32[]{:S(2)}) copy-start(bf16[384,768]{1,0:T(8,128)(2,1)} %copy-done.4) | copy-start | bytes 1769476
Sparse Core Ops, SparseCore 0:
  10.3 55.5 all-gather.7
  68.1 52.4 all-gather.5
  172.2 76.5 reduce-scatter.9
  250.8 86.3 all-gather.9
  341.4 93.2 reduce-scatter.5
  439.3 92.0 reduce-scatter.7
